TPU v7x, 512 devices: a whole 4x8x8 slice. The times are simulated.
512 devices in a mesh: fsdp: 128 (over z, x_lo, y), dp: 4 (over x_hi, core).
Axes of the slice: x: 4 (x_hi: 2, x_lo: 2; x = x_hi * 2 + x_lo), y: 8, z: 8, core: 2. Of those that a mesh axis runs over, the one named last changes fastest.
Arguments:
- glu_input: bfloat16 [131072, 3072], P(('fsdp', 'dp')), may hold values from -6 to 6
- frame_counts: int32 [512, 8], P(('fsdp', 'dp')), may hold values from 1 to 128, as said below
- send_rows: int32 [512, 256], P(('fsdp', 'dp')), may hold values from 0 to 256, as said below
- owner_rows: int32 [512, 160], P(('fsdp', 'dp')), may hold values from 0 to 255, as said below
- depth_kernel: float32 [5, 1536], replicated, may hold values from -2.5 to 2.5
- norm_gain: float32 [1536], replicated, may hold values from 0.25 to 1.75
- norm_bias: float32 [1536], replicated, may hold values from -3 to 3
- point_weight: bfloat16 [1536, 1536], P('fsdp'), may hold values from -0.15625 to 0.15625
- cotangent: bfloat16 [81920, 1536], P(('fsdp', 'dp')), may hold values from -6 to 6
Outputs:
- output: bfloat16 [81920, 1536], P(('fsdp', 'dp'))
- input_grad: bfloat16 [131072, 3072], P(('fsdp', 'dp'))
- kernel_grad: float32 [5, 1536], replicated
- norm_grad: float32 [2, 1536], replicated
Inputs may be any that keep to these rules, and one draw needn't show every extreme that they name: `frame_counts`: A device's counts are the lengths of its 8 utterances. A device's total lies from 64 to 256, both reached at every dp index, and the totals of the devices with one dp index sum to 160 times the fsdp axis size. The longest utterance is reached at every dp index. `send_rows`: entry q of a device's list names the local slot whose activation goes to fsdp index q // 2 with the same dp index, as that owner's position q % 2 from this device; the value 256 marks an unused entry. Each live slot is named once, positions for one owner are used from the lowest up, and some device of every dp index fills all 2 positions for every owner. `owner_rows`: entry b names received position p: position p % 2 from fsdp index p // 2 of the same dp index. The 160 entries are distinct and are exactly the positions that senders use for this owner.
All inputs are finite; a program needn't handle non-finite values.
Results may differ from a plain program's by a relative error of at most 0.0085.
Values may be sent and summed in bfloat16 or wider, within the bound.
No kernel may reach another device: no remote copies, remote signals or barrier semaphores. Data moves between devices by JAX's collectives and lax.ppermute only.
A program may use at most 64 MiB of HBM per device.

v0:
```python
import math
import jax
import jax.numpy as jnp
from jax import lax
from jax.sharding import PartitionSpec as P

eps = 1e-05


def conv_module(glu_rows, counts, kernel, gain_vec, bias_vec):
    row_count = glu_rows.shape[0]
    chan_count = kernel.shape[1]
    half_width = kernel.shape[0] // 2
    values = glu_rows.astype(jnp.float32)
    mixed_vals = values[:, :chan_count] * jax.nn.sigmoid(values[:, chan_count:])
    utter_ends = jnp.cumsum(counts)
    position = jnp.arange(row_count, dtype=jnp.int32)
    segment = jnp.sum((position[:, None] >= utter_ends[None, :]).astype(jnp.int32), axis=1)
    is_live = position < utter_ends[-1]
    mixed_vals = jnp.where(is_live[:, None], mixed_vals, 0.0)
    padded = jnp.pad(mixed_vals, ((half_width, half_width), (0, 0)))
    labels = jnp.pad(segment, (half_width, half_width), constant_values=-1)
    conv_out = jnp.zeros((row_count, chan_count), jnp.float32)
    for offset in range(2 * half_width + 1):
        same_utt = labels[offset : offset + row_count] == segment
        conv_out = (
            conv_out
            + jnp.where(same_utt[:, None], padded[offset : offset + row_count], 0.0)
            * kernel[offset]
        )
    center = jnp.mean(conv_out, axis=1, keepdims=True)
    spread = jnp.mean(jnp.square(conv_out - center), axis=1, keepdims=True)
    normed = (conv_out - center) * lax.rsqrt(spread + eps) * gain_vec + bias_vec
    activated = normed * jax.nn.sigmoid(normed)
    return jnp.where(is_live[:, None], activated, 0.0)


def per_device(
    glu_input,
    frame_counts,
    send_rows,
    owner_rows,
    depth_kernel,
    norm_gain,
    norm_bias,
    point_weight,
    cotangent,
):
    counts = frame_counts[0]
    send_slot = send_rows[0]
    owner_slot = owner_rows[0]
    row_count = glu_input.shape[0]
    out_count = point_weight.shape[1]

    def local_pass(glu_rows, kernel, gain_vec, bias_vec):
        return conv_module(glu_rows, counts, kernel, gain_vec, bias_vec)

    activated, pullback = jax.vjp(local_pass, glu_input, depth_kernel, norm_gain, norm_bias)
    activations = activated.astype(jnp.bfloat16)
    produced = jnp.dot(
        activations,
        lax.all_gather(point_weight, "fsdp", axis=0, tiled=True),
        preferred_element_type=jnp.float32,
    ).astype(jnp.bfloat16)
    outgoing = jnp.concatenate([produced, jnp.zeros((1, out_count), jnp.bfloat16)], axis=0)[
        send_slot
    ]
    arrived = lax.all_to_all(outgoing, "fsdp", split_axis=0, concat_axis=0, tiled=True)
    output = arrived[owner_slot]
    parked = jnp.zeros((row_count, out_count), jnp.bfloat16).at[owner_slot].set(cotangent)
    returned = lax.all_to_all(parked, "fsdp", split_axis=0, concat_axis=0, tiled=True)
    home_rows = (
        jnp.zeros((row_count + 1, out_count), jnp.bfloat16).at[send_slot].set(returned)[:row_count]
    )
    grad_acts = lax.dot_general(
        home_rows,
        lax.all_gather(point_weight, "fsdp", axis=0, tiled=True),
        (((1,), (1,)), ((), ())),
        preferred_element_type=jnp.float32,
    ).astype(jnp.bfloat16)
    input_grad, kernel_part, gain_part, bias_part = pullback(grad_acts.astype(jnp.float32))
    totals = lax.psum((kernel_part, jnp.stack([gain_part, bias_part])), ("fsdp", "dp"))
    frame_total = owner_slot.shape[0] * lax.axis_size("fsdp") * lax.axis_size("dp")
    grad_scale = 1.0 / math.sqrt(frame_total)
    return (output, input_grad, totals[0] * grad_scale, totals[1] * grad_scale)


def solution(mesh):
    in_specs = (
        P(("fsdp", "dp"), None),
        P(("fsdp", "dp"), None),
        P(("fsdp", "dp"), None),
        P(("fsdp", "dp"), None),
        P(),
        P(),
        P(),
        P("fsdp", None),
        P(("fsdp", "dp"), None),
    )
    out_specs = (P(("fsdp", "dp"), None), P(("fsdp", "dp"), None), P(), P())
    return jax.shard_map(
        per_device, mesh=mesh, in_specs=in_specs, out_specs=out_specs, check_vma=False
    )
```

profile of v0, /device:TPU:1, one launch (start us, length us, event | category | flops | bytes accessed | tf_op | source)
XLA Modules:
  0.0 759.5 jit_solution(14914906572277938264)
XLA Ops:
  7.2 0.0 all-gather.3.cloned.1.call-start
  7.2 0.7 all-gather.3.cloned.1.call-update
  7.9 0.7 compare_select_fusion
  8.6 2.1 scatter_custom_fusion
  10.7 0.0 copy-start.10
  10.7 0.0 copy-start.8
  10.7 0.0 copy-start.6
  10.7 1.2 all_to_all.19
  11.9 19.4 %all-to-all-start.1 = ((bf16[128,2,1536]{2,1,0:T(2,128)(2,1)}), bf16[128,2,1536]{2,1,0:T(2,128)(2,1)S(1)}, u32[]{:S(2)}, u32[]{:S(2)}) async-start(bf16[128,2,1536]{2,1,0:T(2,128)(2,1)} %all_to_all.19), calls=%async_computation.1 | async-start | bytes 1572864 | tf_op jit(solution)/shard_map/all_to_all | solution.py:71
  31.3 0.2 reduce-window.4
  31.5 0.6 slice.55
  32.1 0.0 copy-done.8
  32.1 0.1 convert_reduce_fusion
  32.2 0.1 slice_reduce_fusion.4
  32.3 0.1 fusion.21
  32.4 0.7 iota_compare_fusion.1
  33.1 0.3 convert_element_type.24
  33.4 0.0 copy-start
  33.4 0.4 multiply_select_fusion.4
  33.9 1.3 copy-done
  35.2 1.7 fusion.30
  36.9 0.3 multiply_reduce_fusion.7
  37.2 21.3 %all-to-all-done.1 = bf16[128,2,1536]{2,1,0:T(2,128)(2,1)S(1)} async-done(((bf16[128,2,1536]{2,1,0:T(2,128)(2,1)}), bf16[128,2,1536]{2,1,0:T(2,128)(2,1)S(1)}, u32[]{:S(2)}, u32[]{:S(2)}) %all-to-all-start.1) | async-done | bytes 786464 | tf_op jit(solution)/shard_map/all_to_all | solution.py:71
  58.5 0.3 reshape.185
  58.8 2.7 scatter_custom_fusion.1
  61.5 458.1 %all-gather.3.cloned.1.call-done = bf16[128,12,1536]{2,1,0:T(8,128)(2,1)} async-done(((bf16[1,12,1536]{2,1,0:T(8,128)(2,1)}), bf16[128,12,1536]{2,1,0:T(8,128)(2,1)}) %all-gather.3.cloned.1.call-update) | async-done | bytes 4718608 | tf_op jit(solution)/shard_map/all_gather | solution.py:62
  519.6 8.2 %reshape.190 = bf16[1536,1536]{1,0:T(8,128)(2,1)} reshape(bf16[128,12,1536]{2,1,0:T(8,128)(2,1)} %all-gather.3.cloned.1.call-done) | data formatting | bytes 9437184
  527.9 0.0 copy-done.7
  527.9 3.9 convolution_convert_fusion.1
  531.8 0.1 concatenate.3
  531.8 1.3 gather_fusion
  533.1 1.2 all_to_all.16
  534.3 7.4 all-to-all-start
  541.8 4.6 multiply_reduce_fusion
  546.4 0.3 multiply_reduce_fusion.8
  546.7 1.1 copy-done.3
  547.8 2.4 multiply_reduce_fusion.5
  550.2 0.8 multiply_select_fusion.3
  550.9 1.1 copy-done.1
  552.1 1.4 fusion.4
  553.5 0.4 fusion.28
  554.0 192.0 %all-reduce.15 = (f32[5,1536]{1,0:T(8,128)S(1)}, f32[2,1536]{1,0:T(2,128)S(1)}) all-reduce(f32[5,1536]{1,0:T(8,128)S(1)} %pad_add_fusion.4, f32[2,1536]{1,0:T(2,128)S(1)} %pad_maximum_fusion), channel_id=1, replica_groups=mesh['fsdp'=128,'dp'=4] {'fsdp','dp'}, use_global_device_ids=true, to_apply=%region_14.15 | all-reduce | flops 10752 | bytes 86016 | tf_op jit(solution)/shard_map/psum | solution.py:82
  746.1 1.3 add_convert_fusion
  747.4 0.6 broadcast_multiply_fusion.2
  748.0 0.6 broadcast_multiply_fusion.1
  748.6 0.0 all-to-all-done
  748.6 2.3 all_to_all.18
  750.9 1.8 gather_fusion.1
  (29 shorter events, 0.2 us)
Async XLA Ops:
  7.2 512.5 %all-gather.3.cloned.1.call-start = ((), (), s32[]{:S(2)}) async-start(), calls=%async_computation.2 | async-start | bytes 6340608 | tf_op jit(solution)/shard_map/all_gather | solution.py:62
  10.7 20.6 %copy-start.10 = (s32[1,8]{1,0:T(1,128)S(1)}, s32[1,8]{1,0:T(1,128)}, u32[]{:S(2)}) copy-start(s32[1,8]{1,0:T(1,128)} %param.10) | copy-start | bytes 100
  10.7 21.4 %copy-start.8 = (s32[1,256]{1,0:T(1,128)S(1)}, s32[1,256]{1,0:T(1,128)}, u32[]{:S(2)}) copy-start(s32[1,256]{1,0:T(1,128)} %param.11) | copy-start | bytes 3076
  10.7 21.5 %copy-start.6 = (f32[5,1536]{1,0:T(8,128)S(1)}, f32[5,1536]{1,0:T(8,128)}, u32[]{:S(2)}) copy-start(f32[5,1536]{1,0:T(8,128)} %param.13) | copy-start | bytes 92164
  11.9 21.1 %copy-start.4 = (bf16[256,3072]{1,0:T(8,128)(2,1)S(1)}, bf16[256,3072]{1,0:T(8,128)(2,1)}, u32[]{:S(2)}) copy-start(bf16[256,3072]{1,0:T(8,128)(2,1)} %param.9) | copy-start | bytes 4718596
  11.9 46.6 %all-to-all-start.1 = ((bf16[128,2,1536]{2,1,0:T(2,128)(2,1)}), bf16[128,2,1536]{2,1,0:T(2,128)(2,1)S(1)}, u32[]{:S(2)}, u32[]{:S(2)}) async-start(bf16[128,2,1536]{2,1,0:T(2,128)(2,1)} %all_to_all.19), calls=%async_computation.1 | async-start | bytes 1572864 | tf_op jit(solution)/shard_map/all_to_all | solution.py:71
  33.4 1.8 copy-start
  35.2 1.7 copy-start.2
  61.5 466.4 %copy-start.7 = (f32[1536]{0:T(1024)S(1)}, f32[1536]{0:T(1024)}, u32[]{:S(2)}) copy-start(f32[1536]{0:T(1024)} %param.14) | copy-start | bytes 18436
  61.5 466.4 %copy-start.9 = (f32[1536]{0:T(1024)S(1)}, f32[1536]{0:T(1024)}, u32[]{:S(2)}) copy-start(f32[1536]{0:T(1024)} %param.15) | copy-start | bytes 18436
  533.1 8.6 %copy-start.5 = (bf16[257,1536]{1,0:T(8,128)(2,1)S(1)}, bf16[257,1536]{1,0:T(8,128)(2,1)}, u32[]{:S(2)}) copy-start(bf16[257,1536]{1,0:T(8,128)(2,1)} %scatter_custom_fusion.1) | copy-start | bytes 2368516
  534.3 214.3 %all-to-all-start = ((bf16[128,2,1536]{2,1,0:T(2,128)(2,1)}), bf16[128,2,1536]{2,1,0:T(2,128)(2,1)}, u32[]{:S(2)}, u32[]{:S(2)}) async-start(bf16[128,2,1536]{2,1,0:T(2,128)(2,1)} %all_to_all.16), calls=%async_computation | async-start | bytes 1572864 | tf_op jit(solution)/shard_map/all_to_all | solution.py:68
  546.4 1.4 copy-start.3
  550.2 1.9 copy-start.1
Sparse Core Ops, SparseCore 0:
  10.1 509.5 all-gather.2
where the time goes:
time: 760 us
  waiting for transfers between devices  480 us (63%)
  blocking collectives  192 us (25%)
  starting transfers between devices  26.9 us (4%)
  local copies, waits for them, and re-layouts  25.3 us (3%)
  between operations  14.4 us (2%)
  other arithmetic  12.3 us (2%)
  matrix products  8.52 us (1%)
    all_gather x1, waiting for transfers between devices, per_device(): lax.all_gather(point_weight, 'fsdp', axis=0, tiled=True)  458 us
    psum x1, blocking collectives, per_device(): lax.psum((kernel_part, jnp.stack([gain_part, bias_part])), ('fsdp', 'dp'))  192 us
    all_to_all x1, waiting for transfers between devices, per_device(): lax.all_to_all(parked, 'fsdp', split_axis=0, concat_axis=0, tiled=True)  21.3 us
    all_to_all x1, starting transfers between devices, per_device(): lax.all_to_all(parked, 'fsdp', split_axis=0, concat_axis=0, tiled=True)  19.4 us
  transfers between devices with their start and end apart: 3, of which 2 were waited for; matrix products, arithmetic and copies ran while one was open for 3% of the time, Pallas kernels for 0%

commit v1 on v0

--- a/solution.py
+++ b/solution.py
@@ -5,6 +5,9 @@
 from jax.sharding import PartitionSpec as P
 
 eps = 1e-05
+move_chains = lambda shard_in: jnp.concatenate(
+    lax.all_to_all(jnp.stack(lax.axis_size("fsdp") * [shard_in], axis=0), "fsdp", 0, 0), axis=0
+)
 
 
 def conv_module(glu_rows, counts, kernel, gain_vec, bias_vec):
@@ -58,9 +61,7 @@
     activated, pullback = jax.vjp(local_pass, glu_input, depth_kernel, norm_gain, norm_bias)
     activations = activated.astype(jnp.bfloat16)
     produced = jnp.dot(
-        activations,
-        lax.all_gather(point_weight, "fsdp", axis=0, tiled=True),
-        preferred_element_type=jnp.float32,
+        activations, move_chains(point_weight), preferred_element_type=jnp.float32
     ).astype(jnp.bfloat16)
     outgoing = jnp.concatenate([produced, jnp.zeros((1, out_count), jnp.bfloat16)], axis=0)[
         send_slot

time: 760 us -> 836 us (1.10)
  blocking collectives: 192 us -> 230 us
  waiting for transfers between devices: 480 us -> 500 us
  local copies, waits for them, and re-layouts: 25.3 us -> 35.7 us
    all_to_all x1, waiting for transfers between devices: 21.3 us -> 143 us  [lax.all_to_all(jnp.stack(lax.axis_size('fsdp') * [shard_in], axis=0), 'fs...]
    all_gather x1, waiting for transfers between devices: 458 us -> 356 us  [per_device(): lax.all_gather(point_weight, 'fsdp', axis=0, tiled=True)]
    all_to_all x0 -> x1, blocking collectives: none -> 42.7 us  [per_device(): lax.all_to_all(parked, 'fsdp', split_axis=0, concat_axis=0, tiled=True)]
    all_to_all x1, starting transfers between devices: 7.43 us -> 24.2 us  [per_device(): lax.all_to_all(outgoing, 'fsdp', split_axis=0, concat_axis=0, tiled=True)]
    all_to_all x1, starting transfers between devices: 19.4 us -> 8.26 us  [lax.all_to_all(jnp.stack(lax.axis_size('fsdp') * [shard_in], axis=0), 'fs...]
  transfers between devices with their start and end apart: 3 -> 3, of which waited for: 2 -> 2; matrix products, arithmetic and copies ran while one was open for 3% -> 5% of each run, Pallas kernels for 0% -> 0%
where the time goes in v1:
time: 836 us; the launch traced here: 835 us
  waiting for transfers between devices  500 us (60%)
  blocking collectives  230 us (28%)
  local copies, waits for them, and re-layouts  35.7 us (4%)
  starting transfers between devices  32.5 us (4%)
  between operations  14.4 us (2%)
  other arithmetic  13.8 us (2%)
  matrix products  8.49 us (1%)
    all_gather x1, waiting for transfers between devices, per_device(): lax.all_gather(point_weight, 'fsdp', axis=0, tiled=True)  356 us
    psum x1, blocking collectives, per_device(): lax.psum((kernel_part, jnp.stack([gain_part, bias_part])), ('fsdp', 'dp'))  187 us
    all_to_all x1, waiting for transfers between devices, lax.all_to_all(jnp.stack(lax.axis_size('fsdp') * [shard_in], axis=0), 'fs...  143 us
    all_to_all x1, blocking collectives, per_device(): lax.all_to_all(parked, 'fsdp', split_axis=0, concat_axis=0, tiled=True)  42.7 us
    all_to_all x1, starting transfers between devices, per_device(): lax.all_to_all(outgoing, 'fsdp', split_axis=0, concat_axis=0, tiled=True)  24.2 us
  transfers between devices with their start and end apart: 3, of which 2 were waited for; matrix products, arithmetic and copies ran while one was open for 5% of the time, Pallas kernels for 0%

profile of v1, /device:TPU:1, one launch (start us, length us, event | category | flops | bytes accessed | tf_op | source)
XLA Modules:
  0.0 835.0 jit_solution(2222280546742852493)
XLA Ops:
  7.2 0.7 compare_select_fusion
  7.8 2.1 scatter_custom_fusion
  9.9 0.0 copy-start.6
  10.0 0.3 all_to_all.23
  10.3 42.7 %all_to_all.29 = bf16[128,2,1536]{2,1,0:T(2,128)(2,1)} all-to-all(bf16[128,2,1536]{2,1,0:T(2,128)(2,1)S(1)} %all_to_all.23), channel_id=1, replica_groups=mesh['fsdp'=128,'dp'=4] {'fsdp'}, dimensions={0} | all-to-all | bytes 1572864 | tf_op jit(solution)/shard_map/all_to_all | solution.py:72
  53.0 3.4 stack.4
  56.4 8.3 all-to-all-start
  64.6 0.0 all-gather.3.cloned.1.call-start
  64.7 0.7 all-gather.3.cloned.1.call-update
  65.4 0.0 copy-start.11
  65.4 0.0 copy-start.9
  65.4 1.8 convert_element_type.24
  67.2 0.2 reduce-window.4
  67.4 0.8 slice.55
  68.2 0.7 iota_compare_fusion.1
  68.9 0.1 convert_reduce_fusion
  69.0 0.1 slice_reduce_fusion.4
  69.1 0.1 fusion.21
  69.2 0.4 multiply_select_fusion.4
  69.6 0.0 copy-start.2
  69.6 1.7 fusion.30
  71.4 0.3 multiply_reduce_fusion.7
  71.7 0.8 copy-done.4
  72.5 0.3 reshape.191
  72.8 2.7 scatter_custom_fusion.1
  75.5 143.3 %all-to-all-done = bf16[128,12,1536]{2,1,0:T(8,128)(2,1)} async-done(((bf16[128,12,1536]{2,1,0:T(8,128)(2,1)}), bf16[128,12,1536]{2,1,0:T(8,128)(2,1)}, u32[]{:S(2)}, u32[]{:S(2)}) %all-to-all-start) | async-done | bytes 4718624 | tf_op jit(solution)/shard_map/all_to_all | solution.py:9
  218.8 8.2 reshape.155
  227.0 3.9 convolution_convert_fusion.1
  230.9 0.1 concatenate.3
  230.9 1.3 gather_fusion
  232.2 1.2 all_to_all.20
  233.4 24.2 %all-to-all-start.1 = ((bf16[128,2,1536]{2,1,0:T(2,128)(2,1)}), bf16[128,2,1536]{2,1,0:T(2,128)(2,1)}, u32[]{:S(2)}, u32[]{:S(2)}) async-start(bf16[128,2,1536]{2,1,0:T(2,128)(2,1)} %all_to_all.20), calls=%async_computation.1 | async-start | bytes 1572864 | tf_op jit(solution)/shard_map/all_to_all | solution.py:69
  257.7 356.2 %all-gather.3.cloned.1.call-done = bf16[128,12,1536]{2,1,0:T(8,128)(2,1)} async-done(((bf16[1,12,1536]{2,1,0:T(8,128)(2,1)}), bf16[128,12,1536]{2,1,0:T(8,128)(2,1)}) %all-gather.3.cloned.1.call-update) | async-done | bytes 4718608 | tf_op jit(solution)/shard_map/all_gather | solution.py:78
  613.8 8.2 reshape.196
  622.1 4.6 multiply_reduce_fusion
  626.7 0.3 multiply_reduce_fusion.8
  627.0 1.1 copy-done.3
  628.1 2.4 multiply_reduce_fusion.5
  630.5 0.8 multiply_select_fusion.3
  631.2 1.1 copy-done.1
  632.3 1.4 fusion.4
  633.7 0.4 fusion.28
  634.3 187.3 %all-reduce.15 = (f32[5,1536]{1,0:T(8,128)S(1)}, f32[2,1536]{1,0:T(2,128)S(1)}) all-reduce(f32[5,1536]{1,0:T(8,128)S(1)} %pad_add_fusion.4, f32[2,1536]{1,0:T(2,128)S(1)} %pad_maximum_fusion), channel_id=1, replica_groups=mesh['fsdp'=128,'dp'=4] {'fsdp','dp'}, use_global_device_ids=true, to_apply=%region_14.15 | all-reduce | flops 10752 | bytes 86016 | tf_op jit(solution)/shard_map/psum | solution.py:83
  821.6 1.3 add_convert_fusion
  822.9 0.6 broadcast_multiply_fusion.2
  823.5 0.6 broadcast_multiply_fusion.1
  824.1 2.3 all_to_all.22
  826.4 1.8 gather_fusion.1
  (34 shorter events, 0.2 us)
Async XLA Ops:
  9.9 43.0 %copy-start.6 = (bf16[12,1536]{1,0:T(8,128)(2,1)S(1)}, bf16[12,1536]{1,0:T(8,128)(2,1)}, u32[]{:S(2)}) copy-start(bf16[12,1536]{1,0:T(8,128)(2,1)} %param.16) | copy-start | bytes 110596
  56.4 162.5 %all-to-all-start = ((bf16[128,12,1536]{2,1,0:T(8,128)(2,1)}), bf16[128,12,1536]{2,1,0:T(8,128)(2,1)}, u32[]{:S(2)}, u32[]{:S(2)}) async-start(bf16[128,12,1536]{2,1,0:T(8,128)(2,1)} %stack.4), calls=%async_computation | async-start | bytes 12582912 | tf_op jit(solution)/shard_map/all_to_all | solution.py:9
  64.6 549.2 %all-gather.3.cloned.1.call-start = ((), (), s32[]{:S(2)}) async-start(), calls=%async_computation.3 | async-start | bytes 6340608 | tf_op jit(solution)/shard_map/all_gather | solution.py:78
  65.4 1.8 copy-start.11
  65.4 3.5 copy-start.9
  65.4 3.6 copy-start.7
  67.2 2.4 copy-start
  69.6 1.7 copy-start.2
  71.3 1.1 copy-start.4
  75.5 151.5 %copy-start.8 = (f32[1536]{0:T(1024)S(1)}, f32[1536]{0:T(1024)}, u32[]{:S(2)}) copy-start(f32[1536]{0:T(1024)} %param.14) | copy-start | bytes 18436
  75.5 151.5 %copy-start.10 = (f32[1536]{0:T(1024)S(1)}, f32[1536]{0:T(1024)}, u32[]{:S(2)}) copy-start(f32[1536]{0:T(1024)} %param.15) | copy-start | bytes 18436
  233.4 590.8 %all-to-all-start.1 = ((bf16[128,2,1536]{2,1,0:T(2,128)(2,1)}), bf16[128,2,1536]{2,1,0:T(2,128)(2,1)}, u32[]{:S(2)}, u32[]{:S(2)}) async-start(bf16[128,2,1536]{2,1,0:T(2,128)(2,1)} %all_to_all.20), calls=%async_computation.1 | async-start | bytes 1572864 | tf_op jit(solution)/shard_map/all_to_all | solution.py:69
  257.6 364.4 %copy-start.5 = (bf16[257,1536]{1,0:T(8,128)(2,1)S(1)}, bf16[257,1536]{1,0:T(8,128)(2,1)}, u32[]{:S(2)}) copy-start(bf16[257,1536]{1,0:T(8,128)(2,1)} %scatter_custom_fusion.1) | copy-start | bytes 2368516
  626.7 1.4 copy-start.3
  630.5 1.9 copy-start.1
Sparse Core Ops, SparseCore 0:
  67.5 546.2 all-gather.2
